TPU v7x, 32 devices: a whole 2x2x4 slice. The times are simulated.
32 devices in a mesh: groups: 2 (over y), ctx: 4 (over z), sub: 2 (over x), head: 2 (over core).
Axes of the slice: x: 2, y: 2, z: 4, core: 2. Of those that a mesh axis runs over, the one named last changes fastest.
Arguments:
- queries: bfloat16 [32, 10240, 128], P(('sub', 'head'), ('groups', 'ctx')), parts along dimension 1, may hold values from -6 to 6
- keys: bfloat16 [32, 10240, 128], P(('sub', 'head'), ('groups', 'ctx')), parts along dimension 1, may hold values from -6 to 6
- values: bfloat16 [32, 10240, 128], P(('sub', 'head'), ('groups', 'ctx')), parts along dimension 1, may hold values from -90 to 90
- out_grad: bfloat16 [32, 10240, 128], P(('sub', 'head'), ('groups', 'ctx')), parts along dimension 1, may hold values from -6 to 6
- norm_gain: float32 [32, 128], P(('sub', 'head')), may hold values from 0.25 to 1.75
- doc_ids: int32 [40], P(('groups', 'ctx')), parts along dimension 0, may hold values from 0 to 3, never falling along the last dimension, each value on 1 to 10 neighbouring positions
Outputs:
- grad_queries: bfloat16 [32, 10240, 128], P(('sub', 'head'), ('groups', 'ctx')), parts along dimension 1
- grad_keys: bfloat16 [32, 10240, 128], P(('sub', 'head'), ('groups', 'ctx')), parts along dimension 1
- grad_values: bfloat16 [32, 10240, 128], P(('sub', 'head'), ('groups', 'ctx')), parts along dimension 1
There are 2 independent parts, one for each index of `groups`. A program takes and returns all parts, laid end to end along the dimension named above; an argument that names none is the same for every part. Nothing has to cross between parts.
Inputs may be any that keep to these rules, and one draw needn't show every extreme that they name: `doc_ids`: never falls; each of its 4 values labels 1 to 10 consecutive blocks, one value exactly 10.
All inputs are finite; a program needn't handle non-finite values.
Results may differ from a plain program's by a relative error of at most 0.0058.
Values sent between devices are 32-bit elements; how exact they have to be, the bound alone decides.
No kernel may reach another device: no remote copies, remote signals or barrier semaphores. Data moves between devices by JAX's collectives and lax.ppermute only.
A program may use at most 128 MiB of HBM per device.

v0:
```python
import jax
import jax.numpy as jnp
from jax import lax
from jax.sharding import PartitionSpec as P


def segmented_scan(doc, state, axis, reverse):
    peers = lax.axis_size(axis)
    index = lax.axis_index(axis)
    none_doc = jnp.float32(-1.0)

    def shift(value, step):
        if reverse:
            pairs = [(j, j - step) for j in range(step, peers)]
        else:
            pairs = [(j, j + step) for j in range(peers - step)]
        return lax.ppermute(value, axis, pairs)

    def combine(near_doc, near_state, far_doc, far_state):
        joined = (near_doc == far_doc).astype(jnp.float32)
        return (near_doc, near_state + joined * far_state)

    if peers == 1:
        return (none_doc, jnp.zeros_like(state))
    got_doc, got_state = shift((doc, state), 1)
    valid = index >= 1 if not reverse else index <= peers - 2
    ex_doc = jnp.where(valid, got_doc, none_doc)
    ex_state = jnp.where(valid, got_state, 0.0)
    in_doc, in_state = combine(doc, state, ex_doc, ex_state)
    covered = 1
    while covered < peers - 1:
        step = covered + 1
        got_doc, got_state = shift((in_doc, in_state), step)
        valid = index >= step if not reverse else index <= peers - 1 - step
        got_doc = jnp.where(valid, got_doc, none_doc)
        got_state = jnp.where(valid, got_state, 0.0)
        ex_doc, ex_state = combine(ex_doc, ex_state, got_doc, got_state)
        covered = covered + step
        if covered < peers - 1:
            in_doc, in_state = combine(in_doc, in_state, got_doc, got_state)
    return (ex_doc, ex_state)


def on_device(queries, keys, values, out_grad, norm_gain, doc_ids):
    head_count, tok_count, head_width = queries.shape
    block_count = doc_ids.shape[0]
    block_len = tok_count // block_count
    block_shape = (head_count, block_count, block_len, head_width)
    highest_precision = lax.Precision.HIGHEST
    query_blocks = queries.reshape(block_shape)
    key_blocks = keys.reshape(block_shape)
    value_blocks = values.reshape(block_shape)
    row_ids = lax.broadcasted_iota(jnp.int32, (block_len, block_len), 0)
    col_ids = lax.broadcasted_iota(jnp.int32, (block_len, block_len), 1)
    causal = row_ids >= col_ids
    doc_values = doc_ids.astype(jnp.float32)
    block_pos = jnp.arange(block_count, dtype=jnp.int32)
    same_doc = doc_values[:, None] == doc_values[None, :]
    earlier_mask = (same_doc & (block_pos[None, :] < block_pos[:, None])).astype(jnp.float32)
    later_mask = (same_doc & (block_pos[None, :] > block_pos[:, None])).astype(jnp.float32)
    key_value_block = jnp.einsum(
        "hnid,hnie->hnde", key_blocks, value_blocks, preferred_element_type=jnp.float32
    )
    last_match = (doc_values == doc_values[-1]).astype(jnp.float32)
    device_kv = jnp.einsum("c,hcde->hde", last_match, key_value_block, precision=highest_precision)
    prior_doc, prior_state = segmented_scan(doc_values[-1], device_kv, "ctx", False)
    scores = jnp.einsum(
        "hnid,hnjd->hnij", query_blocks, key_blocks, preferred_element_type=jnp.float32
    )
    block_probs = jnp.where(causal, scores, 0.0).astype(jnp.bfloat16)
    intra_part = jnp.einsum(
        "hnij,hnjd->hnid", block_probs, value_blocks, preferred_element_type=jnp.float32
    )
    local_prefix = jnp.einsum(
        "bc,hcde->hbde", earlier_mask, key_value_block, precision=highest_precision
    )
    prior_match = (doc_values == prior_doc).astype(jnp.float32)
    entering = prior_match[None, :, None, None] * prior_state[:, None, :, :]
    preceding_states = (local_prefix + entering).astype(jnp.bfloat16)
    cross_block_part = jnp.einsum(
        "hnid,hnde->hnie", query_blocks, preceding_states, preferred_element_type=jnp.float32
    )
    raw_attn = (intra_part + cross_block_part).reshape(head_count, tok_count, head_width)
    feature_count = head_count * head_width * lax.axis_size(("sub", "head"))
    scaled = norm_gain[:, None, :] * out_grad.astype(jnp.float32)
    local_sums = jnp.stack(
        [jnp.sum(raw_attn * raw_attn, axis=(0, 2)), jnp.sum(scaled * raw_attn, axis=(0, 2))]
    )
    total_sums = lax.psum(local_sums, ("sub", "head"))
    root_mean = jnp.sqrt(total_sums[0] / feature_count + 1e-06)
    inner_mean = total_sums[1] / feature_count
    factor = inner_mean / (root_mean * root_mean)
    d_attn = ((scaled - raw_attn * factor[None, :, None]) / root_mean[None, :, None]).astype(
        jnp.bfloat16
    )
    output_grad_blocks = d_attn.reshape(block_shape)
    query_grad_block = jnp.einsum(
        "hnid,hnie->hnde", query_blocks, output_grad_blocks, preferred_element_type=jnp.float32
    )
    first_match = (doc_values == doc_values[0]).astype(jnp.float32)
    device_qd = jnp.einsum(
        "c,hcde->hde", first_match, query_grad_block, precision=highest_precision
    )
    next_doc, next_state = segmented_scan(doc_values[0], device_qd, "ctx", True)
    grad_scores = jnp.einsum(
        "hnid,hnjd->hnij", output_grad_blocks, value_blocks, preferred_element_type=jnp.float32
    )
    grad_probs = jnp.where(causal, grad_scores, 0.0).astype(jnp.bfloat16)
    query_gradient = jnp.einsum(
        "hnij,hnjd->hnid", grad_probs, key_blocks, preferred_element_type=jnp.float32
    )
    key_gradient = jnp.einsum(
        "hnij,hnid->hnjd", grad_probs, query_blocks, preferred_element_type=jnp.float32
    )
    value_gradient = jnp.einsum(
        "hnij,hnid->hnjd", block_probs, output_grad_blocks, preferred_element_type=jnp.float32
    )
    local_suffix = jnp.einsum(
        "bc,hcde->hbde", later_mask, query_grad_block, precision=highest_precision
    )
    next_match = (doc_values == next_doc).astype(jnp.float32)
    leaving = next_match[None, :, None, None] * next_state[:, None, :, :]
    following_states = (local_suffix + leaving).astype(jnp.bfloat16)
    query_gradient = query_gradient + jnp.einsum(
        "hnie,hnde->hnid", output_grad_blocks, preceding_states, preferred_element_type=jnp.float32
    )
    key_gradient = key_gradient + jnp.einsum(
        "hnie,hnde->hnid", value_blocks, following_states, preferred_element_type=jnp.float32
    )
    value_gradient = value_gradient + jnp.einsum(
        "hnid,hnde->hnie", key_blocks, following_states, preferred_element_type=jnp.float32
    )
    out_shape = (head_count, tok_count, head_width)
    return (
        query_gradient.reshape(out_shape).astype(jnp.bfloat16),
        key_gradient.reshape(out_shape).astype(jnp.bfloat16),
        value_gradient.reshape(out_shape).astype(jnp.bfloat16),
    )


def solution(mesh):
    return jax.shard_map(
        on_device,
        mesh=mesh,
        in_specs=(
            P(("sub", "head"), ("groups", "ctx"), None),
            P(("sub", "head"), ("groups", "ctx"), None),
            P(("sub", "head"), ("groups", "ctx"), None),
            P(("sub", "head"), ("groups", "ctx"), None),
            P(("sub", "head"), None),
            P(("groups", "ctx")),
        ),
        out_specs=(
            P(("sub", "head"), ("groups", "ctx"), None),
            P(("sub", "head"), ("groups", "ctx"), None),
            P(("sub", "head"), ("groups", "ctx"), None),
        ),
        check_vma=False,
    )
```

profile of v0, /device:TPU:0, one launch (start us, length us, event | category | flops | bytes accessed | tf_op | source)
XLA Modules:
  0.0 159.0 jit_solution(8993034932632156992)
XLA Ops:
  4.6 7.6 %collective-permute-start.2 = (f32[]{:T(128)}, f32[]{:T(128)}, u32[]{:S(2)}, u32[]{:S(2)}) collective-permute-start(f32[]{:T(128)} %bitcast.7), channel_id=1, source_target_pairs={{0,8},{4,12},{1,9},{5,13},{2,10},{6,14},{3,11},{7,15},{16,24},{20,... | collective-permute-start | bytes 20 | tf_op jit(solution)/shard_map/ppermute | solution.py:17
  12.2 5.0 %collective-permute-start = (f32[]{:T(128)}, f32[]{:T(128)}, u32[]{:S(2)}, u32[]{:S(2)}) collective-permute-start(f32[]{:T(128)} %bitcast.7), channel_id=1, source_target_pairs={{0,4},{4,8},{8,12},{1,5},{5,9},{9,13},{2,6},{6,10},{10,14},{3,7},{... | collective-permute-start | bytes 20 | tf_op jit(solution)/shard_map/ppermute | solution.py:17
  17.2 3.4 %fusion.36 = f32[8,5,128,128]{3,2,1,0:T(8,128)S(1)} fusion(bf16[8,5,256,128]{3,2,1,0:T(8,128)(2,1)} %bitcast.105, bf16[8,5,256,128]{3,2,1,0:T(8,128)(2,1)} %bitcast.109), kind=kOutput, calls=%fused_computation.62 | convolution fusion | flops 335544320 | bytes 7864320 | tf_op jit(solution)/shard_map/hnid,hnie->hnde/dot_general | solution.py:61
  22.1 4.9 %fusion.6 = f32[1,8,128,128]{3,0,2,1:T(1,128)} fusion(f32[8,5,128,128]{3,2,1,0:T(8,128)S(1)} %fusion.36, f32[]{:T(128)} %bitcast.7, s32[5]{0:T(128)S(1)} %copy-done.16), kind=kOutput, calls=%fused_computation.16 | convolution fusion | flops 7864330 | bytes 3145752 | tf_op jit(solution)/shard_map/c,hcde->hde/dot_general | solution.py:65
  28.5 3.4 %select_convert_fusion.1 = bf16[8,5,256,256]{3,2,1,0:T(8,128)(2,1)S(1)} fusion(pred[256,256]{1,0:T(8,128)(4,1)S(1)} %iota_compare_fusion, bf16[8,5,256,128]{3,2,1,0:T(8,128)(2,1)S(1)} %bitcast.95, bf16[8,5,256,128]{3,2,1,0:T(8,128)(2,1)} %bitcast.106), kind=kOutput, calls=%fused_computation.1 | convolution fusion | flops 676331520 | bytes 10551296 | tf_op jit(solution)/shard_map/hnid,hnjd->hnij/dot_general | solution.py:67
  31.9 4.0 %fusion.35 = f32[8,5,256,128]{3,2,1,0:T(8,128)} fusion(bf16[8,5,256,256]{3,2,1,0:T(8,128)(2,1)S(1)} %select_convert_fusion.1, bf16[8,5,256,128]{3,2,1,0:T(8,128)(2,1)S(1)} %bitcast.110), kind=kOutput, calls=%fused_computation.61 | convolution fusion | flops 671088640 | bytes 13107200 | tf_op jit(solution)/shard_map/hnij,hnjd->hnid/dot_general | solution.py:71
  37.2 2.1 %collective-permute-done.1 = f32[8,128,128]{2,1,0:T(8,128)S(1)} collective-permute-done((f32[8,128,128]{2,1,0:T(8,128)}, f32[8,128,128]{2,1,0:T(8,128)S(1)}, u32[]{:S(2)}, u32[]{:S(2)}) %collective-permute-start.1) | collective-permute-done | bytes 524320 | tf_op jit(solution)/shard_map/ppermute | solution.py:17
  41.2 4.8 %collective-permute-start.3 = (f32[8,128,128]{2,1,0:T(8,128)}, f32[8,128,128]{2,1,0:T(8,128)}, u32[]{:S(2)}, u32[]{:S(2)}) collective-permute-start(f32[8,128,128]{2,1,0:T(8,128)} %multiply_add_fusion.3), channel_id=1, source_target_pairs={{0,8},{4,12},{1,9},{5,13},{2,10},{6,14},{3,11},{7,15},{16,24},{20,... | collective-permute-start | bytes 1572872 | tf_op jit(solution)/shard_map/ppermute | solution.py:17
  46.0 7.2 %fusion.8 = f32[8,128,128,5]{2,3,1,0:T(8,128)} fusion(f32[8,5,128,128]{3,2,1,0:T(8,128)} %copy-done.2, f32[5]{0:T(128)S(1)} %convert_element_type.63), kind=kOutput, calls=%fused_computation.18 | convolution fusion | flops 39321676 | bytes 5242900 | tf_op jit(solution)/shard_map/bc,hcde->hbde/dot_general | solution.py:74
  55.8 3.0 %fusion.11 = bf16[8,5,128,128]{3,2,1,0:T(8,128)(2,1)S(1)} fusion(f32[8,128,128,5]{2,3,1,0:T(8,128)} %fusion.8, f32[8,128,128]{2,1,0:T(8,128)S(1)} %multiply_add_fusion.2, f32[5]{0:T(128)S(1)} %get-tuple-element.6), kind=kLoop, calls=%fused_computation.23 | loop fusion | flops 1966080 | bytes 4456468 | tf_op jit(solution)/shard_map/convert_element_type | solution.py:79
  63.1 10.3 %psum.7 = f32[2,1280]{1,0:T(2,128)S(1)} all-reduce(f32[2,1280]{1,0:T(2,128)S(1)} %pad_maximum_fusion), channel_id=1, replica_groups=mesh['groups'=2,'ctx'=4,'sub'=2,'head'=2] {'sub','head'}, use_global_device_ids=true, to_apply=%region_2.3 | all-reduce | flops 2560 | bytes 20480 | tf_op jit(solution)/shard_map/psum | solution.py:89
  73.5 4.0 %fusion.5 = bf16[8,1280,128]{2,1,0:T(8,128)(2,1)S(1)} fusion(f32[8,5,256,128]{3,2,1,0:T(8,128)} %copy-done.1, bf16[8,1280,128]{2,1,0:T(8,128)(2,1)} %param.9, f32[1280]{0:T(1024)S(1)} %get-tuple-element.4, f32[1280]{0:T(1024)S(1)} %multiply_divide_fusion, f32[8,128]{1,0:T(8,128)S(1)} %copy-done.15), kind=kLoop, calls=%fused_computation.11 | loop fusion | flops 7864320 | bytes 10500096 | tf_op jit(solution)/shard_map/convert_element_type | solution.py:93
  77.5 7.4 %fusion.39 = f32[8,5,256,128]{3,2,1,0:T(8,128)} fusion(bf16[8,5,256,256]{3,2,1,0:T(8,128)(2,1)} %copy-done.6, bf16[8,5,256,128]{3,2,1,0:T(8,128)(2,1)S(1)} %bitcast.99), kind=kOutput, calls=%fused_computation.65 | convolution fusion | flops 671088640 | bytes 13107200 | tf_op jit(solution)/shard_map/hnij,hnid->hnjd/dot_general | solution.py:115
  84.9 2.4 %convolution_bitcast_fusion = f32[8,5,128,128]{2,3,1,0:T(8,128)} fusion(bf16[8,5,256,128]{3,2,1,0:T(8,128)(2,1)S(1)} %bitcast.100, bf16[8,5,256,128]{3,2,1,0:T(8,128)(2,1)S(1)} %bitcast.98), kind=kOutput, calls=%fused_computation.24 | convolution fusion | flops 335544320 | bytes 7864320 | tf_op jit(solution)/shard_map/hnid,hnie->hnde/dot_general | solution.py:97
  87.3 3.9 %select_convert_fusion = bf16[8,5,256,256]{3,2,1,0:T(8,128)(2,1)} fusion(pred[256,256]{1,0:T(8,128)(4,1)S(1)} %iota_compare_fusion, bf16[8,5,256,128]{3,2,1,0:T(8,128)(2,1)S(1)} %bitcast.101, bf16[8,5,256,128]{3,2,1,0:T(8,128)(2,1)S(1)} %bitcast.111), kind=kOutput, calls=%fused_computation | convolution fusion | flops 676331520 | bytes 10551296 | tf_op jit(solution)/shard_map/hnid,hnjd->hnij/dot_general | solution.py:105
  91.2 4.7 %copy.29 = f32[8,5,128,128]{3,1,2,0:T(8,128)} copy(f32[8,5,128,128]{2,3,1,0:T(8,128)} %convolution_bitcast_fusion) | data formatting | bytes 5242880 | tf_op jit(solution)/shard_map/hnid,hnie->hnde/dot_general | solution.py:97
  95.9 5.2 %fusion.25 = f32[1,8,128,128]{3,0,2,1:T(1,128)S(1)} fusion(f32[8,5,128,128]{3,1,2,0:T(8,128)} %copy.29, f32[]{:T(128)} %bitcast.21, s32[5]{0:T(128)S(1)} %copy-done.16), kind=kOutput, calls=%fused_computation.49 | convolution fusion | flops 7864330 | bytes 3145752 | tf_op jit(solution)/shard_map/c,hcde->hde/dot_general | solution.py:101
  102.5 4.2 %fusion.38 = f32[8,5,256,128]{3,2,1,0:T(8,128)S(1)} fusion(bf16[8,5,256,256]{3,2,1,0:T(8,128)(2,1)} %select_convert_fusion, bf16[8,5,256,128]{3,2,1,0:T(8,128)(2,1)S(1)} %bitcast.97), kind=kOutput, calls=%fused_computation.64 | convolution fusion | flops 671088640 | bytes 13107200 | tf_op jit(solution)/shard_map/hnij,hnid->hnjd/dot_general | solution.py:112
  108.3 17.3 %collective-permute-done.5 = f32[8,128,128]{2,1,0:T(8,128)S(1)} collective-permute-done((f32[8,128,128]{2,1,0:T(8,128)S(1)}, f32[8,128,128]{2,1,0:T(8,128)S(1)}, u32[]{:S(2)}, u32[]{:S(2)}) %collective-permute-start.5) | collective-permute-done | bytes 524320 | tf_op jit(solution)/shard_map/ppermute | solution.py:17
  127.5 2.2 %fusion.19 = f32[8,128,128,5]{2,3,1,0:T(8,128)S(1)} fusion(f32[8,5,128,128]{3,1,2,0:T(8,128)S(1)} %copy-done.5, f32[5]{0:T(128)S(1)} %convert_element_type.63), kind=kOutput, calls=%fused_computation.44 | convolution fusion | flops 39321676 | bytes 5242900 | tf_op jit(solution)/shard_map/bc,hcde->hbde/dot_general | solution.py:118
  129.7 2.4 %add_convert_fusion = bf16[8,5,256,128]{3,2,1,0:T(8,128)(2,1)} fusion(f32[8,5,256,128]{3,2,1,0:T(8,128)S(1)} %fusion.37, bf16[8,5,256,128]{3,2,1,0:T(8,128)(2,1)S(1)} %bitcast.102, bf16[8,5,128,128]{3,2,1,0:T(8,128)(2,1)S(1)} %copy-done.13), kind=kOutput, calls=%fused_computation.13 | convolution fusion | flops 338165760 | bytes 11796480 | tf_op jit(solution)/shard_map/hnie,hnde->hnid/dot_general | solution.py:124
  132.2 21.3 %collective-permute-done.7 = f32[8,128,128]{2,1,0:T(8,128)S(1)} collective-permute-done((f32[8,128,128]{2,1,0:T(8,128)S(1)}, f32[8,128,128]{2,1,0:T(8,128)S(1)}, u32[]{:S(2)}, u32[]{:S(2)}) %collective-permute-start.7) | collective-permute-done | bytes 524320 | tf_op jit(solution)/shard_map/ppermute | solution.py:17
  154.2 2.4 %fusion = bf16[8,5,256,128]{3,2,1,0:T(8,128)(2,1)} fusion(f32[8,5,256,128]{3,2,1,0:T(8,128)S(1)} %bitcast.114, bf16[8,5,256,128]{3,2,1,0:T(8,128)(2,1)S(1)} %bitcast.108, bf16[8,5,128,128]{3,2,1,0:T(8,128)(2,1)S(1)} %fusion.10), kind=kOutput, calls=%fused_computation.3 | convolution fusion | flops 338165760 | bytes 11796480 | tf_op jit(solution)/shard_map/hnid,hnde->hnie/dot_general | solution.py:130
  156.6 2.4 %fusion.1 = bf16[8,5,256,128]{3,2,1,0:T(8,128)(2,1)} fusion(f32[8,5,256,128]{3,2,1,0:T(8,128)S(1)} %fusion.38, bf16[8,5,128,128]{3,2,1,0:T(8,128)(2,1)S(1)} %fusion.10, bf16[8,5,256,128]{3,2,1,0:T(8,128)(2,1)S(1)} %bitcast.112), kind=kOutput, calls=%fused_computation.5 | convolution fusion | flops 338165760 | bytes 11796480 | tf_op jit(solution)/shard_map/hnie,hnde->hnid/dot_general | solution.py:127
  (71 shorter events, 18.8 us)
Async XLA Ops:
  0.6 27.8 %copy-start = (bf16[8,1280,128]{2,1,0:T(8,128)(2,1)S(1)}, bf16[8,1280,128]{2,1,0:T(8,128)(2,1)}, u32[]{:S(2)}) copy-start(bf16[8,1280,128]{2,1,0:T(8,128)(2,1)} %param.6) | copy-start | bytes 7864324
  2.0 52.4 %collective-permute-start.6 = (f32[]{:T(128)}, f32[]{:T(128)}, u32[]{:S(2)}, u32[]{:S(2)}) collective-permute-start(f32[]{:T(128)} %bitcast.21), channel_id=1, source_target_pairs={{8,0},{12,4},{9,1},{13,5},{10,2},{14,6},{11,3},{15,7},{24,16},{28,... | collective-permute-start | bytes 20 | tf_op jit(solution)/shard_map/ppermute | solution.py:17
  3.3 49.9 %collective-permute-start.4 = (f32[]{:T(128)}, f32[]{:T(128)}, u32[]{:S(2)}, u32[]{:S(2)}) collective-permute-start(f32[]{:T(128)} %bitcast.21), channel_id=1, source_target_pairs={{4,0},{8,4},{12,8},{5,1},{9,5},{13,9},{6,2},{10,6},{14,10},{7,3},{... | collective-permute-start | bytes 20 | tf_op jit(solution)/shard_map/ppermute | solution.py:17
  4.6 50.5 %collective-permute-start.2 = (f32[]{:T(128)}, f32[]{:T(128)}, u32[]{:S(2)}, u32[]{:S(2)}) collective-permute-start(f32[]{:T(128)} %bitcast.7), channel_id=1, source_target_pairs={{0,8},{4,12},{1,9},{5,13},{2,10},{6,14},{3,11},{7,15},{16,24},{20,... | collective-permute-start | bytes 20 | tf_op jit(solution)/shard_map/ppermute | solution.py:17
  12.2 23.7 %collective-permute-start = (f32[]{:T(128)}, f32[]{:T(128)}, u32[]{:S(2)}, u32[]{:S(2)}) collective-permute-start(f32[]{:T(128)} %bitcast.7), channel_id=1, source_target_pairs={{0,4},{4,8},{8,12},{1,5},{5,9},{9,13},{2,6},{6,10},{10,14},{3,7},{... | collective-permute-start | bytes 20 | tf_op jit(solution)/shard_map/ppermute | solution.py:17
  17.2 4.9 %copy-start.16 = (s32[5]{0:T(128)S(1)}, s32[5]{0:T(128)}, u32[]{:S(2)}) copy-start(s32[5]{0:T(128)} %param.11) | copy-start | bytes 64
  27.0 12.3 %collective-permute-start.1 = (f32[8,128,128]{2,1,0:T(8,128)}, f32[8,128,128]{2,1,0:T(8,128)S(1)}, u32[]{:S(2)}, u32[]{:S(2)}) collective-permute-start(f32[8,128,128]{2,1,0:T(8,128)} %bitcast.11), channel_id=1, source_target_pairs={{0,4},{4,8},{8,12},{1,5},{5,9},{9,13},{2,6},{6,10},{10,14},{3,7},{... | collective-permute-start | bytes 1572872 | tf_op jit(solution)/shard_map/ppermute | solution.py:17
  28.5 3.4 %copy-start.9 = (bf16[8,1280,128]{2,1,0:T(8,128)(2,1)S(1)}, bf16[8,1280,128]{2,1,0:T(8,128)(2,1)}, u32[]{:S(2)}) copy-start(bf16[8,1280,128]{2,1,0:T(8,128)(2,1)} %param.8) | copy-start | bytes 7864324
  31.9 4.0 %copy-start.6 = (bf16[8,5,256,256]{3,2,1,0:T(8,128)(2,1)}, bf16[8,5,256,256]{3,2,1,0:T(8,128)(2,1)S(1)}, u32[]{:S(2)}) copy-start(bf16[8,5,256,256]{3,2,1,0:T(8,128)(2,1)S(1)} %select_convert_fusion.1) | copy-start | bytes 15728644
  41.2 14.5 %collective-permute-start.3 = (f32[8,128,128]{2,1,0:T(8,128)}, f32[8,128,128]{2,1,0:T(8,128)}, u32[]{:S(2)}, u32[]{:S(2)}) collective-permute-start(f32[8,128,128]{2,1,0:T(8,128)} %multiply_add_fusion.3), channel_id=1, source_target_pairs={{0,8},{4,12},{1,9},{5,13},{2,10},{6,14},{3,11},{7,15},{16,24},{20,... | collective-permute-start | bytes 1572872 | tf_op jit(solution)/shard_map/ppermute | solution.py:17
  55.8 3.7 %copy-start.7 = (f32[8,5,256,128]{3,2,1,0:T(8,128)S(1)}, f32[8,5,256,128]{3,2,1,0:T(8,128)}, u32[]{:S(2)}) copy-start(f32[8,5,256,128]{3,2,1,0:T(8,128)} %fusion.35) | copy-start | bytes 15728644
  77.5 9.8 %copy-start.3 = (bf16[8,1280,128]{2,1,0:T(8,128)(2,1)}, bf16[8,1280,128]{2,1,0:T(8,128)(2,1)S(1)}, u32[]{:S(2)}) copy-start(bf16[8,1280,128]{2,1,0:T(8,128)(2,1)S(1)} %fusion.5) | copy-start | bytes 7864324
  84.9 2.4 %copy-start.10 = (bf16[8,1280,128]{2,1,0:T(8,128)(2,1)S(1)}, bf16[8,1280,128]{2,1,0:T(8,128)(2,1)}, u32[]{:S(2)}) copy-start(bf16[8,1280,128]{2,1,0:T(8,128)(2,1)} %param.8) | copy-start | bytes 7864324
  95.9 10.9 %slice-start = ((s8[5242880]{0:T(1024)(128)(4,1)}), s8[4194304]{0:T(1024)(128)(4,1)S(1)}, s32[]{:S(2)}) async-start(s8[5242880]{0:T(1024)(128)(4,1)} %bitcast.103), calls=%async_computation | async-start | bytes 8388608
  101.1 5.7 %slice-start.1 = ((s8[5242880]{0:T(1024)(128)(4,1)}), s8[1048576]{0:T(1024)(128)(4,1)S(1)}, s32[]{:S(2)}) async-start(s8[5242880]{0:T(1024)(128)(4,1)} %bitcast.103), calls=%async_computation.1 | async-start | bytes 2097152
  101.1 24.5 %collective-permute-start.5 = (f32[8,128,128]{2,1,0:T(8,128)S(1)}, f32[8,128,128]{2,1,0:T(8,128)S(1)}, u32[]{:S(2)}, u32[]{:S(2)}) collective-permute-start(f32[8,128,128]{2,1,0:T(8,128)S(1)} %bitcast.118), channel_id=1, source_target_pairs={{4,0},{8,4},{12,8},{5,1},{9,5},{13,9},{6,2},{10,6},{14,10},{7,3},{... | collective-permute-start | bytes 1572872 | tf_op jit(solution)/shard_map/ppermute | solution.py:17
  102.5 4.2 %copy-start.8 = (bf16[8,1280,128]{2,1,0:T(8,128)(2,1)S(1)}, bf16[8,1280,128]{2,1,0:T(8,128)(2,1)}, u32[]{:S(2)}) copy-start(bf16[8,1280,128]{2,1,0:T(8,128)(2,1)} %param.7) | copy-start | bytes 7864324
  106.8 20.7 %copy-start.5 = (f32[8,5,128,128]{3,1,2,0:T(8,128)S(1)}, f32[8,5,128,128]{3,1,2,0:T(8,128)}, u32[]{:S(2)}) copy-start(f32[8,5,128,128]{3,1,2,0:T(8,128)} %copy.29) | copy-start | bytes 7864324
  125.6 4.1 %copy-start.4 = (bf16[8,1280,128]{2,1,0:T(8,128)(2,1)S(1)}, bf16[8,1280,128]{2,1,0:T(8,128)(2,1)}, u32[]{:S(2)}) copy-start(bf16[8,1280,128]{2,1,0:T(8,128)(2,1)} %copy-done.3) | copy-start | bytes 7864324
  125.6 4.1 %copy-start.13 = (bf16[8,5,128,128]{3,2,1,0:T(8,128)(2,1)S(1)}, bf16[8,5,128,128]{3,2,1,0:T(8,128)(2,1)}, u32[]{:S(2)}) copy-start(bf16[8,5,128,128]{3,2,1,0:T(8,128)(2,1)} %copy-done.12) | copy-start | bytes 3932164
  125.6 27.8 %collective-permute-start.7 = (f32[8,128,128]{2,1,0:T(8,128)S(1)}, f32[8,128,128]{2,1,0:T(8,128)S(1)}, u32[]{:S(2)}, u32[]{:S(2)}) collective-permute-start(f32[8,128,128]{2,1,0:T(8,128)S(1)} %multiply_add_fusion.1), channel_id=1, source_target_pairs={{8,0},{12,4},{9,1},{13,5},{10,2},{14,6},{11,3},{15,7},{24,16},{28,... | collective-permute-start | bytes 1572872 | tf_op jit(solution)/shard_map/ppermute | solution.py:17
  127.5 26.7 %slice-start.2 = ((s8[5242880]{0:T(1024)(128)(4,1)}), s8[4194304]{0:T(1024)(128)(4,1)S(1)}, s32[]{:S(2)}) async-start(s8[5242880]{0:T(1024)(128)(4,1)} %bitcast.113), calls=%async_computation.2 | async-start | bytes 8388608
  129.7 24.5 %slice-start.3 = ((s8[5242880]{0:T(1024)(128)(4,1)}), s8[1048576]{0:T(1024)(128)(4,1)S(1)}, s32[]{:S(2)}) async-start(s8[5242880]{0:T(1024)(128)(4,1)} %bitcast.113), calls=%async_computation.3 | async-start | bytes 2097152
  154.2 2.4 %copy-start.11 = (bf16[8,1280,128]{2,1,0:T(8,128)(2,1)S(1)}, bf16[8,1280,128]{2,1,0:T(8,128)(2,1)}, u32[]{:S(2)}) copy-start(bf16[8,1280,128]{2,1,0:T(8,128)(2,1)} %param.8) | copy-start | bytes 7864324
  (5 other events, 9.7 us)
where the time goes:
time: 160 us; the launch traced here: 159 us
  matrix products  58.1 us (36%)
  waiting for transfers between devices  40.7 us (25%)
  starting transfers between devices  24.5 us (15%)
  other arithmetic  11.4 us (7%)
  blocking collectives  10.3 us (6%)
  local copies, waits for them, and re-layouts  9.19 us (6%)
  between operations  4.79 us (3%)
    ppermute x8, waiting for transfers between devices, shift(): return lax.ppermute(value, axis, pairs)  40.7 us
    ppermute x8, starting transfers between devices, shift(): return lax.ppermute(value, axis, pairs)  24.5 us
    psum x1, blocking collectives, on_device(): total_sums = lax.psum(local_sums, ('sub', 'head'))  10.3 us
    dot_general x1, matrix products, on_device(): jnp.einsum('hnij,hnid->hnjd', block_probs, output_grad_blocks, preferred_...  7.37 us
    dot_general x1, matrix products, on_device(): jnp.einsum('bc,hcde->hbde', earlier_mask, key_value_block, precision=high...  7.22 us
    dot_general x1, matrix products, on_device(): jnp.einsum('c,hcde->hde', first_match, query_grad_block, precision=highes...  5.18 us
    dot_general x1, matrix products, on_device(): jnp.einsum('c,hcde->hde', last_match, key_value_block, precision=highest_...  4.89 us
    dot_general x1, local copies, waits for them, and re-layouts, on_device(): jnp.einsum('hnid,hnie->hnde', query_blocks, output_grad_blocks, preferred...  4.7 us
  transfers between devices with their start and end apart: 8, of which 3 were waited for; matrix products, arithmetic and copies ran while one was open for 22% of the time, Pallas kernels for 0%

commit v1 on v0

--- a/solution.py
+++ b/solution.py
@@ -86,7 +86,8 @@
     local_sums = jnp.stack(
         [jnp.sum(raw_attn * raw_attn, axis=(0, 2)), jnp.sum(scaled * raw_attn, axis=(0, 2))]
     )
-    total_sums = lax.psum(local_sums, ("sub", "head"))
+    blocks = lax.all_gather(local_sums, ("sub", "head"))
+    total_sums = jnp.sum(blocks, axis=0)
     root_mean = jnp.sqrt(total_sums[0] / feature_count + 1e-06)
     inner_mean = total_sums[1] / feature_count
     factor = inner_mean / (root_mean * root_mean)

time: 160 us -> 156 us (0.975)
  blocking collectives: 10.3 us -> 5.63 us
    psum x1 -> x0, blocking collectives: 10.3 us -> none  [on_device(): total_sums = lax.psum(local_sums, ('sub', 'head'))]
    all_gather x0 -> x1, blocking collectives: none -> 5.63 us  [on_device(): blocks = lax.all_gather(local_sums, ('sub', 'head'))]
  transfers between devices with their start and end apart: 8 -> 8, of which waited for: 3 -> 3; matrix products, arithmetic and copies ran while one was open for 22% -> 23% of each run, Pallas kernels for 0% -> 0%
where the time goes in v1:
time: 156 us; the launch traced here: 155 us
  matrix products  58.1 us (37%)
  waiting for transfers between devices  41.8 us (27%)
  starting transfers between devices  24.5 us (16%)
  other arithmetic  11.4 us (7%)
  local copies, waits for them, and re-layouts  9.19 us (6%)
  blocking collectives  5.63 us (4%)
  between operations  4.79 us (3%)
    ppermute x8, waiting for transfers between devices, shift(): return lax.ppermute(value, axis, pairs)  41.8 us
    ppermute x8, starting transfers between devices, shift(): return lax.ppermute(value, axis, pairs)  24.5 us
    dot_general x1, matrix products, on_device(): jnp.einsum('hnij,hnid->hnjd', block_probs, output_grad_blocks, preferred_...  7.38 us
    dot_general x1, matrix products, on_device(): jnp.einsum('bc,hcde->hbde', earlier_mask, key_value_block, precision=high...  7.22 us
    all_gather x1, blocking collectives, on_device(): blocks = lax.all_gather(local_sums, ('sub', 'head'))  5.63 us
    dot_general x1, matrix products, on_device(): jnp.einsum('c,hcde->hde', first_match, query_grad_block, precision=highes...  5.18 us
    dot_general x1, matrix products, on_device(): jnp.einsum('c,hcde->hde', last_match, key_value_block, precision=highest_...  4.89 us
    dot_general x1, local copies, waits for them, and re-layouts, on_device(): jnp.einsum('hnid,hnie->hnde', query_blocks, output_grad_blocks, preferred...  4.7 us
  transfers between devices with their start and end apart: 8, of which 3 were waited for; matrix products, arithmetic and copies ran while one was open for 23% of the time, Pallas kernels for 0%

profile of v1, /device:TPU:0, one launch (start us, length us, event | category | flops | bytes accessed | tf_op | source)
XLA Modules:
  0.0 155.5 jit_solution(3425827465993729216)
XLA Ops:
  4.6 7.6 %collective-permute-start.2 = (f32[]{:T(128)}, f32[]{:T(128)}, u32[]{:S(2)}, u32[]{:S(2)}) collective-permute-start(f32[]{:T(128)} %bitcast.7), channel_id=1, source_target_pairs={{0,8},{4,12},{1,9},{5,13},{2,10},{6,14},{3,11},{7,15},{16,24},{20,... | collective-permute-start | bytes 20 | tf_op jit(solution)/shard_map/ppermute | solution.py:17
  12.2 5.0 %collective-permute-start = (f32[]{:T(128)}, f32[]{:T(128)}, u32[]{:S(2)}, u32[]{:S(2)}) collective-permute-start(f32[]{:T(128)} %bitcast.7), channel_id=1, source_target_pairs={{0,4},{4,8},{8,12},{1,5},{5,9},{9,13},{2,6},{6,10},{10,14},{3,7},{... | collective-permute-start | bytes 20 | tf_op jit(solution)/shard_map/ppermute | solution.py:17
  17.2 3.4 %fusion.36 = f32[8,5,128,128]{3,2,1,0:T(8,128)S(1)} fusion(bf16[8,5,256,128]{3,2,1,0:T(8,128)(2,1)} %bitcast.107, bf16[8,5,256,128]{3,2,1,0:T(8,128)(2,1)} %bitcast.111), kind=kOutput, calls=%fused_computation.62 | convolution fusion | flops 335544320 | bytes 7864320 | tf_op jit(solution)/shard_map/hnid,hnie->hnde/dot_general | solution.py:61
  22.1 4.9 %fusion.6 = f32[1,8,128,128]{3,0,2,1:T(1,128)} fusion(f32[8,5,128,128]{3,2,1,0:T(8,128)S(1)} %fusion.36, f32[]{:T(128)} %bitcast.7, s32[5]{0:T(128)S(1)} %copy-done.16), kind=kOutput, calls=%fused_computation.16 | convolution fusion | flops 7864330 | bytes 3145752 | tf_op jit(solution)/shard_map/c,hcde->hde/dot_general | solution.py:65
  28.5 3.4 %select_convert_fusion.1 = bf16[8,5,256,256]{3,2,1,0:T(8,128)(2,1)S(1)} fusion(pred[256,256]{1,0:T(8,128)(4,1)S(1)} %iota_compare_fusion, bf16[8,5,256,128]{3,2,1,0:T(8,128)(2,1)S(1)} %bitcast.97, bf16[8,5,256,128]{3,2,1,0:T(8,128)(2,1)} %bitcast.108), kind=kOutput, calls=%fused_computation.1 | convolution fusion | flops 676331520 | bytes 10551296 | tf_op jit(solution)/shard_map/hnid,hnjd->hnij/dot_general | solution.py:67
  31.9 4.0 %fusion.35 = f32[8,5,256,128]{3,2,1,0:T(8,128)} fusion(bf16[8,5,256,256]{3,2,1,0:T(8,128)(2,1)S(1)} %select_convert_fusion.1, bf16[8,5,256,128]{3,2,1,0:T(8,128)(2,1)S(1)} %bitcast.112), kind=kOutput, calls=%fused_computation.61 | convolution fusion | flops 671088640 | bytes 13107200 | tf_op jit(solution)/shard_map/hnij,hnjd->hnid/dot_general | solution.py:71
  37.2 2.1 %collective-permute-done.1 = f32[8,128,128]{2,1,0:T(8,128)S(1)} collective-permute-done((f32[8,128,128]{2,1,0:T(8,128)}, f32[8,128,128]{2,1,0:T(8,128)S(1)}, u32[]{:S(2)}, u32[]{:S(2)}) %collective-permute-start.1) | collective-permute-done | bytes 524320 | tf_op jit(solution)/shard_map/ppermute | solution.py:17
  41.2 4.8 %collective-permute-start.3 = (f32[8,128,128]{2,1,0:T(8,128)}, f32[8,128,128]{2,1,0:T(8,128)}, u32[]{:S(2)}, u32[]{:S(2)}) collective-permute-start(f32[8,128,128]{2,1,0:T(8,128)} %multiply_add_fusion.3), channel_id=1, source_target_pairs={{0,8},{4,12},{1,9},{5,13},{2,10},{6,14},{3,11},{7,15},{16,24},{20,... | collective-permute-start | bytes 1572872 | tf_op jit(solution)/shard_map/ppermute | solution.py:17
  46.0 7.2 %fusion.8 = f32[8,128,128,5]{2,3,1,0:T(8,128)} fusion(f32[8,5,128,128]{3,2,1,0:T(8,128)} %copy-done.2, f32[5]{0:T(128)S(1)} %convert_element_type.63), kind=kOutput, calls=%fused_computation.18 | convolution fusion | flops 39321676 | bytes 5242900 | tf_op jit(solution)/shard_map/bc,hcde->hbde/dot_general | solution.py:74
  55.8 3.0 %fusion.11 = bf16[8,5,128,128]{3,2,1,0:T(8,128)(2,1)S(1)} fusion(f32[8,128,128,5]{2,3,1,0:T(8,128)} %fusion.8, f32[8,128,128]{2,1,0:T(8,128)S(1)} %multiply_add_fusion.2, f32[5]{0:T(128)S(1)} %get-tuple-element.6), kind=kLoop, calls=%fused_computation.23 | loop fusion | flops 1966080 | bytes 4456468 | tf_op jit(solution)/shard_map/convert_element_type | solution.py:79
  63.1 5.6 %all-gather.1 = f32[4,2,1280]{2,1,0:T(2,128)S(1)} all-gather(f32[1,2,1280]{2,1,0:T(2,128)S(1)} %maximum_bitcast_fusion), channel_id=2, replica_groups=mesh['groups'=2,'ctx'=4,'sub'=2,'head'=2] {'sub','head'}, dimensions={0}, use_global_device_ids=true | all-gather | bytes 51200 | tf_op jit(solution)/shard_map/all_gather | solution.py:89
  68.8 4.0 %fusion.5 = bf16[8,1280,128]{2,1,0:T(8,128)(2,1)S(1)} fusion(f32[8,5,256,128]{3,2,1,0:T(8,128)} %copy-done.1, bf16[8,1280,128]{2,1,0:T(8,128)(2,1)} %param.9, f32[1280]{0:T(1024)S(1)} %get-tuple-element.4, f32[1280]{0:T(1024)S(1)} %multiply_divide_fusion, f32[8,128]{1,0:T(8,128)S(1)} %copy-done.15), kind=kLoop, calls=%fused_computation.11 | loop fusion | flops 7864320 | bytes 10500096 | tf_op jit(solution)/shard_map/convert_element_type | solution.py:94
  72.9 7.4 %fusion.39 = f32[8,5,256,128]{3,2,1,0:T(8,128)} fusion(bf16[8,5,256,256]{3,2,1,0:T(8,128)(2,1)} %copy-done.6, bf16[8,5,256,128]{3,2,1,0:T(8,128)(2,1)S(1)} %bitcast.101), kind=kOutput, calls=%fused_computation.65 | convolution fusion | flops 671088640 | bytes 13107200 | tf_op jit(solution)/shard_map/hnij,hnid->hnjd/dot_general | solution.py:116
  80.2 2.4 %convolution_bitcast_fusion = f32[8,5,128,128]{2,3,1,0:T(8,128)} fusion(bf16[8,5,256,128]{3,2,1,0:T(8,128)(2,1)S(1)} %bitcast.102, bf16[8,5,256,128]{3,2,1,0:T(8,128)(2,1)S(1)} %bitcast.100), kind=kOutput, calls=%fused_computation.24 | convolution fusion | flops 335544320 | bytes 7864320 | tf_op jit(solution)/shard_map/hnid,hnie->hnde/dot_general | solution.py:98
  82.6 3.9 %select_convert_fusion = bf16[8,5,256,256]{3,2,1,0:T(8,128)(2,1)} fusion(pred[256,256]{1,0:T(8,128)(4,1)S(1)} %iota_compare_fusion, bf16[8,5,256,128]{3,2,1,0:T(8,128)(2,1)S(1)} %bitcast.103, bf16[8,5,256,128]{3,2,1,0:T(8,128)(2,1)S(1)} %bitcast.113), kind=kOutput, calls=%fused_computation | convolution fusion | flops 676331520 | bytes 10551296 | tf_op jit(solution)/shard_map/hnid,hnjd->hnij/dot_general | solution.py:106
  86.5 4.7 %copy.42 = f32[8,5,128,128]{3,1,2,0:T(8,128)} copy(f32[8,5,128,128]{2,3,1,0:T(8,128)} %convolution_bitcast_fusion) | data formatting | bytes 5242880 | tf_op jit(solution)/shard_map/hnid,hnie->hnde/dot_general | solution.py:98
  91.2 5.2 %fusion.25 = f32[1,8,128,128]{3,0,2,1:T(1,128)S(1)} fusion(f32[8,5,128,128]{3,1,2,0:T(8,128)} %copy.42, f32[]{:T(128)} %bitcast.22, s32[5]{0:T(128)S(1)} %copy-done.16), kind=kOutput, calls=%fused_computation.49 | convolution fusion | flops 7864330 | bytes 3145752 | tf_op jit(solution)/shard_map/c,hcde->hde/dot_general | solution.py:102
  97.8 4.2 %fusion.38 = f32[8,5,256,128]{3,2,1,0:T(8,128)S(1)} fusion(bf16[8,5,256,256]{3,2,1,0:T(8,128)(2,1)} %select_convert_fusion, bf16[8,5,256,128]{3,2,1,0:T(8,128)(2,1)S(1)} %bitcast.99), kind=kOutput, calls=%fused_computation.64 | convolution fusion | flops 671088640 | bytes 13107200 | tf_op jit(solution)/shard_map/hnij,hnid->hnjd/dot_general | solution.py:113
  103.6 17.7 %collective-permute-done.5 = f32[8,128,128]{2,1,0:T(8,128)S(1)} collective-permute-done((f32[8,128,128]{2,1,0:T(8,128)S(1)}, f32[8,128,128]{2,1,0:T(8,128)S(1)}, u32[]{:S(2)}, u32[]{:S(2)}) %collective-permute-start.5) | collective-permute-done | bytes 524320 | tf_op jit(solution)/shard_map/ppermute | solution.py:17
  123.2 2.2 %fusion.19 = f32[8,128,128,5]{2,3,1,0:T(8,128)S(1)} fusion(f32[8,5,128,128]{3,1,2,0:T(8,128)S(1)} %copy-done.5, f32[5]{0:T(128)S(1)} %convert_element_type.63), kind=kOutput, calls=%fused_computation.44 | convolution fusion | flops 39321676 | bytes 5242900 | tf_op jit(solution)/shard_map/bc,hcde->hbde/dot_general | solution.py:119
  125.5 2.4 %add_convert_fusion = bf16[8,5,256,128]{3,2,1,0:T(8,128)(2,1)} fusion(f32[8,5,256,128]{3,2,1,0:T(8,128)S(1)} %fusion.37, bf16[8,5,256,128]{3,2,1,0:T(8,128)(2,1)S(1)} %bitcast.104, bf16[8,5,128,128]{3,2,1,0:T(8,128)(2,1)S(1)} %copy-done.13), kind=kOutput, calls=%fused_computation.13 | convolution fusion | flops 338165760 | bytes 11796480 | tf_op jit(solution)/shard_map/hnie,hnde->hnid/dot_general | solution.py:125
  127.9 22.0 %collective-permute-done.7 = f32[8,128,128]{2,1,0:T(8,128)S(1)} collective-permute-done((f32[8,128,128]{2,1,0:T(8,128)S(1)}, f32[8,128,128]{2,1,0:T(8,128)S(1)}, u32[]{:S(2)}, u32[]{:S(2)}) %collective-permute-start.7) | collective-permute-done | bytes 524320 | tf_op jit(solution)/shard_map/ppermute | solution.py:17
  150.7 2.4 %fusion = bf16[8,5,256,128]{3,2,1,0:T(8,128)(2,1)} fusion(f32[8,5,256,128]{3,2,1,0:T(8,128)S(1)} %bitcast.116, bf16[8,5,256,128]{3,2,1,0:T(8,128)(2,1)S(1)} %bitcast.110, bf16[8,5,128,128]{3,2,1,0:T(8,128)(2,1)S(1)} %fusion.10), kind=kOutput, calls=%fused_computation.3 | convolution fusion | flops 338165760 | bytes 11796480 | tf_op jit(solution)/shard_map/hnid,hnde->hnie/dot_general | solution.py:131
  153.0 2.4 %fusion.1 = bf16[8,5,256,128]{3,2,1,0:T(8,128)(2,1)} fusion(f32[8,5,256,128]{3,2,1,0:T(8,128)S(1)} %fusion.38, bf16[8,5,128,128]{3,2,1,0:T(8,128)(2,1)S(1)} %fusion.10, bf16[8,5,256,128]{3,2,1,0:T(8,128)(2,1)S(1)} %bitcast.114), kind=kOutput, calls=%fused_computation.5 | convolution fusion | flops 338165760 | bytes 11796480 | tf_op jit(solution)/shard_map/hnie,hnde->hnid/dot_general | solution.py:128
  (72 shorter events, 18.9 us)
Async XLA Ops:
  0.6 27.8 %copy-start = (bf16[8,1280,128]{2,1,0:T(8,128)(2,1)S(1)}, bf16[8,1280,128]{2,1,0:T(8,128)(2,1)}, u32[]{:S(2)}) copy-start(bf16[8,1280,128]{2,1,0:T(8,128)(2,1)} %param.6) | copy-start | bytes 7864324
  2.0 52.4 %collective-permute-start.6 = (f32[]{:T(128)}, f32[]{:T(128)}, u32[]{:S(2)}, u32[]{:S(2)}) collective-permute-start(f32[]{:T(128)} %bitcast.22), channel_id=1, source_target_pairs={{8,0},{12,4},{9,1},{13,5},{10,2},{14,6},{11,3},{15,7},{24,16},{28,... | collective-permute-start | bytes 20 | tf_op jit(solution)/shard_map/ppermute | solution.py:17
  3.3 49.9 %collective-permute-start.4 = (f32[]{:T(128)}, f32[]{:T(128)}, u32[]{:S(2)}, u32[]{:S(2)}) collective-permute-start(f32[]{:T(128)} %bitcast.22), channel_id=1, source_target_pairs={{4,0},{8,4},{12,8},{5,1},{9,5},{13,9},{6,2},{10,6},{14,10},{7,3},{... | collective-permute-start | bytes 20 | tf_op jit(solution)/shard_map/ppermute | solution.py:17
  4.6 50.5 %collective-permute-start.2 = (f32[]{:T(128)}, f32[]{:T(128)}, u32[]{:S(2)}, u32[]{:S(2)}) collective-permute-start(f32[]{:T(128)} %bitcast.7), channel_id=1, source_target_pairs={{0,8},{4,12},{1,9},{5,13},{2,10},{6,14},{3,11},{7,15},{16,24},{20,... | collective-permute-start | bytes 20 | tf_op jit(solution)/shard_map/ppermute | solution.py:17
  12.2 23.7 %collective-permute-start = (f32[]{:T(128)}, f32[]{:T(128)}, u32[]{:S(2)}, u32[]{:S(2)}) collective-permute-start(f32[]{:T(128)} %bitcast.7), channel_id=1, source_target_pairs={{0,4},{4,8},{8,12},{1,5},{5,9},{9,13},{2,6},{6,10},{10,14},{3,7},{... | collective-permute-start | bytes 20 | tf_op jit(solution)/shard_map/ppermute | solution.py:17
  17.2 4.9 %copy-start.16 = (s32[5]{0:T(128)S(1)}, s32[5]{0:T(128)}, u32[]{:S(2)}) copy-start(s32[5]{0:T(128)} %param.11) | copy-start | bytes 64
  27.0 12.3 %collective-permute-start.1 = (f32[8,128,128]{2,1,0:T(8,128)}, f32[8,128,128]{2,1,0:T(8,128)S(1)}, u32[]{:S(2)}, u32[]{:S(2)}) collective-permute-start(f32[8,128,128]{2,1,0:T(8,128)} %bitcast.11), channel_id=1, source_target_pairs={{0,4},{4,8},{8,12},{1,5},{5,9},{9,13},{2,6},{6,10},{10,14},{3,7},{... | collective-permute-start | bytes 1572872 | tf_op jit(solution)/shard_map/ppermute | solution.py:17
  28.5 3.4 %copy-start.9 = (bf16[8,1280,128]{2,1,0:T(8,128)(2,1)S(1)}, bf16[8,1280,128]{2,1,0:T(8,128)(2,1)}, u32[]{:S(2)}) copy-start(bf16[8,1280,128]{2,1,0:T(8,128)(2,1)} %param.8) | copy-start | bytes 7864324
  31.9 4.0 %copy-start.6 = (bf16[8,5,256,256]{3,2,1,0:T(8,128)(2,1)}, bf16[8,5,256,256]{3,2,1,0:T(8,128)(2,1)S(1)}, u32[]{:S(2)}) copy-start(bf16[8,5,256,256]{3,2,1,0:T(8,128)(2,1)S(1)} %select_convert_fusion.1) | copy-start | bytes 15728644
  41.2 14.5 %collective-permute-start.3 = (f32[8,128,128]{2,1,0:T(8,128)}, f32[8,128,128]{2,1,0:T(8,128)}, u32[]{:S(2)}, u32[]{:S(2)}) collective-permute-start(f32[8,128,128]{2,1,0:T(8,128)} %multiply_add_fusion.3), channel_id=1, source_target_pairs={{0,8},{4,12},{1,9},{5,13},{2,10},{6,14},{3,11},{7,15},{16,24},{20,... | collective-permute-start | bytes 1572872 | tf_op jit(solution)/shard_map/ppermute | solution.py:17
  55.8 3.7 %copy-start.7 = (f32[8,5,256,128]{3,2,1,0:T(8,128)S(1)}, f32[8,5,256,128]{3,2,1,0:T(8,128)}, u32[]{:S(2)}) copy-start(f32[8,5,256,128]{3,2,1,0:T(8,128)} %fusion.35) | copy-start | bytes 15728644
  72.9 9.8 %copy-start.3 = (bf16[8,1280,128]{2,1,0:T(8,128)(2,1)}, bf16[8,1280,128]{2,1,0:T(8,128)(2,1)S(1)}, u32[]{:S(2)}) copy-start(bf16[8,1280,128]{2,1,0:T(8,128)(2,1)S(1)} %fusion.5) | copy-start | bytes 7864324
  80.2 2.4 %copy-start.10 = (bf16[8,1280,128]{2,1,0:T(8,128)(2,1)S(1)}, bf16[8,1280,128]{2,1,0:T(8,128)(2,1)}, u32[]{:S(2)}) copy-start(bf16[8,1280,128]{2,1,0:T(8,128)(2,1)} %param.8) | copy-start | bytes 7864324
  91.2 10.9 %slice-start = ((s8[5242880]{0:T(1024)(128)(4,1)}), s8[4194304]{0:T(1024)(128)(4,1)S(1)}, s32[]{:S(2)}) async-start(s8[5242880]{0:T(1024)(128)(4,1)} %bitcast.105), calls=%async_computation | async-start | bytes 8388608
  96.4 5.7 %slice-start.1 = ((s8[5242880]{0:T(1024)(128)(4,1)}), s8[1048576]{0:T(1024)(128)(4,1)S(1)}, s32[]{:S(2)}) async-start(s8[5242880]{0:T(1024)(128)(4,1)} %bitcast.105), calls=%async_computation.1 | async-start | bytes 2097152
  96.4 24.9 %collective-permute-start.5 = (f32[8,128,128]{2,1,0:T(8,128)S(1)}, f32[8,128,128]{2,1,0:T(8,128)S(1)}, u32[]{:S(2)}, u32[]{:S(2)}) collective-permute-start(f32[8,128,128]{2,1,0:T(8,128)S(1)} %bitcast.120), channel_id=1, source_target_pairs={{4,0},{8,4},{12,8},{5,1},{9,5},{13,9},{6,2},{10,6},{14,10},{7,3},{... | collective-permute-start | bytes 1572872 | tf_op jit(solution)/shard_map/ppermute | solution.py:17
  97.8 4.2 %copy-start.8 = (bf16[8,1280,128]{2,1,0:T(8,128)(2,1)S(1)}, bf16[8,1280,128]{2,1,0:T(8,128)(2,1)}, u32[]{:S(2)}) copy-start(bf16[8,1280,128]{2,1,0:T(8,128)(2,1)} %param.7) | copy-start | bytes 7864324
  102.1 21.1 %copy-start.5 = (f32[8,5,128,128]{3,1,2,0:T(8,128)S(1)}, f32[8,5,128,128]{3,1,2,0:T(8,128)}, u32[]{:S(2)}) copy-start(f32[8,5,128,128]{3,1,2,0:T(8,128)} %copy.42) | copy-start | bytes 7864324
  121.4 4.1 %copy-start.4 = (bf16[8,1280,128]{2,1,0:T(8,128)(2,1)S(1)}, bf16[8,1280,128]{2,1,0:T(8,128)(2,1)}, u32[]{:S(2)}) copy-start(bf16[8,1280,128]{2,1,0:T(8,128)(2,1)} %copy-done.3) | copy-start | bytes 7864324
  121.4 4.1 %copy-start.13 = (bf16[8,5,128,128]{3,2,1,0:T(8,128)(2,1)S(1)}, bf16[8,5,128,128]{3,2,1,0:T(8,128)(2,1)}, u32[]{:S(2)}) copy-start(bf16[8,5,128,128]{3,2,1,0:T(8,128)(2,1)} %copy-done.12) | copy-start | bytes 3932164
  121.4 28.5 %collective-permute-start.7 = (f32[8,128,128]{2,1,0:T(8,128)S(1)}, f32[8,128,128]{2,1,0:T(8,128)S(1)}, u32[]{:S(2)}, u32[]{:S(2)}) collective-permute-start(f32[8,128,128]{2,1,0:T(8,128)S(1)} %multiply_add_fusion.1), channel_id=1, source_target_pairs={{8,0},{12,4},{9,1},{13,5},{10,2},{14,6},{11,3},{15,7},{24,16},{28,... | collective-permute-start | bytes 1572872 | tf_op jit(solution)/shard_map/ppermute | solution.py:17
  123.2 27.4 %slice-start.2 = ((s8[5242880]{0:T(1024)(128)(4,1)}), s8[4194304]{0:T(1024)(128)(4,1)S(1)}, s32[]{:S(2)}) async-start(s8[5242880]{0:T(1024)(128)(4,1)} %bitcast.115), calls=%async_computation.2 | async-start | bytes 8388608
  125.5 25.2 %slice-start.3 = ((s8[5242880]{0:T(1024)(128)(4,1)}), s8[1048576]{0:T(1024)(128)(4,1)S(1)}, s32[]{:S(2)}) async-start(s8[5242880]{0:T(1024)(128)(4,1)} %bitcast.115), calls=%async_computation.3 | async-start | bytes 2097152
  150.6 2.4 %copy-start.11 = (bf16[8,1280,128]{2,1,0:T(8,128)(2,1)S(1)}, bf16[8,1280,128]{2,1,0:T(8,128)(2,1)}, u32[]{:S(2)}) copy-start(bf16[8,1280,128]{2,1,0:T(8,128)(2,1)} %param.8) | copy-start | bytes 7864324
  (5 other events, 9.7 us)
